TPU v7x, 128 devices: a whole 4x4x4 slice. The times are simulated.
128 devices in a mesh: feat: 8 (over y, core), dom: 16 (over z, x).
Axes of the slice: x: 4, y: 4, z: 4, core: 2. Of those that a mesh axis runs over, the one named last changes fastest.
Arguments:
- features: bfloat16 [768, 262144], P('feat', 'dom'), may hold values from -6 to 6
- neighbours: int32 [65536, 15], P('dom'), may hold values from 0 to 16383
- self_first: bfloat16 [768, 1024], replicated, may hold values from -0.21875 to 0.21875
- neighbour_first: bfloat16 [768, 1024], replicated, may hold values from -0.21875 to 0.21875
- owners: int32 [655360, 1], P(('feat', 'dom')), may hold values from 0 to 15; in each aligned block of 5120 rows (0 to 5119, 5120 to 10239, ...) at most 400 rows name the same one
- offsets: int32 [65536, 10], P(('feat', 'dom')), may hold values from 0 to 511
- self_second: bfloat16 [1024, 1024], replicated, may hold values from -0.1875 to 0.1875
- neighbour_second: bfloat16 [1024, 1024], replicated, may hold values from -0.1875 to 0.1875
- cotangent: bfloat16 [65536, 1024], P(('feat', 'dom')), may hold values from -0.0234375 to 0.0234375
Outputs:
- second_out: bfloat16 [65536, 1024], P(('feat', 'dom'))
- grad_self_second: float32 [1024, 1024], replicated
- grad_neighbour_second: float32 [1024, 1024], replicated
Inputs may be any that keep to these rules, and one draw needn't show every extreme that they name: `owners`: among the 5120 slots of one device (rows of one device), no partition is named more than 400 times, a bound that some block reaches.
All inputs are finite; a program needn't handle non-finite values.
Results may differ from a plain program's by a relative error of at most 0.007.
Values may be sent and summed in bfloat16 or wider, within the bound.
No kernel may reach another device: no remote copies, remote signals or barrier semaphores. Data moves between devices by JAX's collectives and lax.ppermute only.
A program may use at most 192 MiB of HBM per device.

v0:
```python
import jax
import jax.numpy as jnp
from jax import lax
from jax.sharding import PartitionSpec as P


def contract(left, right):
    return lax.dot_general(
        left, right, (((0,), (0,)), ((), ())), preferred_element_type=jnp.float32
    )


def shards(
    features,
    neighbours,
    self_first,
    neighbour_first,
    owners,
    offsets,
    self_second,
    neighbour_second,
    cotangent,
):
    columns_here = features.shape[0]
    targets_part = neighbours.shape[0]
    fanout_first = neighbours.shape[1]
    hidden_width = self_first.shape[1]
    feat_size = lax.axis_size("feat")
    share_rows = targets_part // feat_size
    node_rows = features.T
    gathered = jnp.take(node_rows, neighbours.reshape(-1), axis=0, mode="clip")
    mixed_rows = (
        jnp.sum(
            gathered.reshape(targets_part, fanout_first, columns_here), axis=1, dtype=jnp.float32
        )
        / fanout_first
    ).astype(jnp.bfloat16)
    own_rows = node_rows[:targets_part]
    both = jnp.stack([own_rows, mixed_rows], axis=1).reshape(feat_size, share_rows, 2, columns_here)
    arrived = lax.all_to_all(both, "feat", 0, 0, tiled=True)
    lhs = jnp.transpose(arrived, (1, 0, 2, 3)).reshape(share_rows, -1)
    weights = jnp.stack(
        [
            self_first.reshape(feat_size, columns_here, hidden_width),
            neighbour_first.reshape(feat_size, columns_here, hidden_width),
        ],
        axis=1,
    ).reshape(-1, hidden_width)
    pre_first = jnp.dot(lhs, weights, preferred_element_type=jnp.float32)
    layer_out = jnp.maximum(pre_first, 0.0).astype(jnp.bfloat16)
    seed_rows = cotangent.shape[0]
    fanout_second = offsets.shape[1]
    segment = lax.all_gather(layer_out, "dom", axis=0, tiled=True)
    flat_rows = owners.reshape(seed_rows, fanout_second) * share_rows + offsets
    fetched = jnp.take(segment, flat_rows.reshape(-1), axis=0, mode="clip")
    summed = jnp.sum(
        fetched.reshape(seed_rows, fanout_second, hidden_width), axis=1, dtype=jnp.float32
    )
    mean_second = (summed / fanout_second).astype(jnp.bfloat16)
    second_out = (
        jnp.dot(layer_out, self_second, preferred_element_type=jnp.float32)
        + jnp.dot(mean_second, neighbour_second, preferred_element_type=jnp.float32)
    ).astype(jnp.bfloat16)
    grad_self = contract(layer_out, cotangent)
    grad_neighbour = contract(mean_second, cotangent)
    grad_self, grad_neighbour = lax.psum((grad_self, grad_neighbour), ("feat", "dom"))
    return (second_out, grad_self, grad_neighbour)


def solution(mesh):
    placed = (
        P("feat", "dom"),
        P("dom", None),
        P(),
        P(),
        P(("feat", "dom"), None),
        P(("feat", "dom"), None),
        P(),
        P(),
        P(("feat", "dom"), None),
    )
    return jax.shard_map(
        shards,
        mesh=mesh,
        in_specs=placed,
        out_specs=(P(("feat", "dom"), None), P(), P()),
        check_vma=False,
    )
```

profile of v0, /device:TPU:1, one launch (start us, length us, event | category | flops | bytes accessed | tf_op | source)
XLA Modules:
  0.0 679.6 jit_solution(10008456262759413801)
XLA Ops:
  7.2 0.0 copy-start
  7.2 0.0 all-gather.2.cloned.1.call-start
  7.2 3.0 copy.28
  10.3 3.2 reshape.46
  13.5 5.9 copy.26
  19.4 1.3 slice.8
  20.7 1.2 copy.30
  21.9 208.3 %gather_fusion = bf16[61440,96]{1,0:T(8,128)(2,1)} fusion(bf16[16384,96]{1,0:T(8,128)(2,1)} %bitcast.25, s32[61440]{0:T(1024)S(1)} %broadcast_clamp_fusion), kind=kCustom, calls=%fused_computation | custom fusion | bytes 23838720 | tf_op jit(solution)/shard_map/jit(_take)/gather | solution.py:31
  230.3 26.1 %reshape.42 = f32[4096,15,96]{2,1,0:T(8,128)} reshape(bf16[61440,96]{1,0:T(8,128)(2,1)} %gather_fusion) | data formatting | bytes 35389440 | tf_op jit(solution)/shard_map/convert_element_type | solution.py:33
  256.3 25.2 %reduce_sum.18 = f32[4096,96]{1,0:T(8,128)} reduce(f32[4096,15,96]{2,1,0:T(8,128)} %reshape.42, f32[]{:T(128)} %constant.4.clone.1), dimensions={1}, to_apply=%region_0.1 | reduce | flops 5505024 | bytes 25165828 | tf_op jit(solution)/shard_map/reduce_sum | solution.py:33
  281.5 2.8 copy.29
  284.3 1.5 multiply_convert_fusion.1
  285.8 0.0 copy-start.4
  285.8 0.3 copy.36
  286.1 0.2 copy.31
  286.4 0.6 copy-done.4
  287.0 0.1 pad_maximum_fusion
  287.1 0.0 copy-start.8
  287.1 0.0 copy-start.9
  287.1 26.6 %all_to_all.5 = bf16[8,512,2,96]{1,3,2,0:T(8,128)(2,1)S(1)} all-to-all(bf16[8,512,2,96]{1,3,2,0:T(8,128)(2,1)S(1)} %pad_maximum_fusion), channel_id=1, replica_groups=mesh['feat'=8,'dom'=16] {'feat'}, dimensions={0} | all-to-all | bytes 3145728 | tf_op jit(solution)/shard_map/all_to_all | solution.py:40
  313.7 0.0 copy-done.8
  313.7 0.0 copy-done.9
  313.7 2.8 fusion.4
  316.5 0.0 all-gather.2.cloned.1.call-update
  316.5 0.2 all-reduce.3.cloned.1.call-start
  316.8 0.0 copy-done.6
  316.8 0.1 multiply_reduce_fusion
  316.8 0.2 mul.11
  317.1 0.0 copy-done.5
  317.1 0.9 copy.32
  317.9 1.7 add.10
  319.6 1.1 reshape.54
  320.7 0.0 copy-done.2
  320.8 4.5 fusion.13
  325.3 103.3 %all-gather.2.cloned.1.call-done = bf16[8192,1024]{1,0:T(8,128)(2,1)} async-done(((bf16[512,1024]{1,0:T(8,128)(2,1)}), bf16[8192,1024]{1,0:T(8,128)(2,1)}) %all-gather.2.cloned.1.call-update) | async-done | bytes 16777232 | tf_op jit(solution)/shard_map/all_gather | solution.py:53
  428.6 33.7 %gather_fusion.1 = bf16[5120,1024]{1,0:T(8,128)(2,1)} fusion(bf16[8192,1024]{1,0:T(8,128)(2,1)} %all-gather.2.cloned.1.call-done, s32[5120]{0:T(1024)S(1)} %broadcast_clamp_fusion.1), kind=kCustom, calls=%fused_computation.1 | custom fusion | bytes 20992000 | tf_op jit(solution)/shard_map/jit(_take)/gather | solution.py:55
  462.3 21.4 %reshape.43 = f32[512,10,1024]{2,1,0:T(8,128)} reshape(bf16[5120,1024]{1,0:T(8,128)(2,1)} %gather_fusion.1) | data formatting | bytes 31457280 | tf_op jit(solution)/shard_map/convert_element_type | solution.py:56
  483.7 15.6 %reduce_sum.19 = f32[512,1024]{1,0:T(8,128)} reduce(f32[512,10,1024]{2,1,0:T(8,128)} %reshape.43, f32[]{:T(128)} %constant.4.clone.1), dimensions={1}, to_apply=%region_1.2 | reduce | flops 4718592 | bytes 23068676 | tf_op jit(solution)/shard_map/reduce_sum | solution.py:56
  499.3 5.2 fusion.8
  504.4 0.0 all-reduce.3.cloned.1.call-update
  504.5 0.0 copy-start.7
  504.5 1.3 fusion.12
  505.7 0.3 copy-done.1
  506.1 0.6 copy-done.7
  506.7 2.2 add_convert_fusion
  508.9 156.8 %all-reduce.3.cloned.1.call-done = (f32[1024,1024]{1,0:T(8,128)}, f32[1024,1024]{1,0:T(8,128)}) async-done(((f32[1024,1024]{1,0:T(8,128)}, f32[1024,1024]{1,0:T(8,128)}), (f32[1024,1024]{1,0:T(8,128)}, f32[1024,1024]{1,0:T(8,128)})) %all-reduce.3.cloned.1.call-update) | async-done | bytes 8388624 | tf_op jit(solution)/shard_map/psum | solution.py:66
  665.8 4.9 copy.39
  670.7 2.0 copy.40
  (9 shorter events, 0.1 us)
Async XLA Ops:
  7.2 497.3 %copy-start = (bf16[1024,1024]{1,0:T(8,128)(2,1)S(1)}, bf16[1024,1024]{1,0:T(8,128)(2,1)}, u32[]{:S(2)}) copy-start(bf16[1024,1024]{1,0:T(8,128)(2,1)} %param.15) | copy-start | bytes 6291460
  7.2 421.4 %all-gather.2.cloned.1.call-start = ((), (), s32[]{:S(2)}) async-start(), calls=%async_computation.1 | async-start | bytes 17825792 | tf_op jit(solution)/shard_map/all_gather | solution.py:53
  285.8 1.1 copy-start.4
  287.1 26.6 %copy-start.8 = (bf16[768,1024]{1,0:T(8,128)(2,1)S(1)}, bf16[768,1024]{1,0:T(8,128)(2,1)}, u32[]{:S(2)}) copy-start(bf16[768,1024]{1,0:T(8,128)(2,1)} %param.12) | copy-start | bytes 4718596
  287.1 26.6 %copy-start.9 = (bf16[768,1024]{1,0:T(8,128)(2,1)S(1)}, bf16[768,1024]{1,0:T(8,128)(2,1)}, u32[]{:S(2)}) copy-start(bf16[768,1024]{1,0:T(8,128)(2,1)} %param.11) | copy-start | bytes 4718596
  313.7 3.1 copy-start.6
  313.7 3.4 copy-start.5
  316.5 4.2 copy-start.2
  316.5 349.2 %all-reduce.3.cloned.1.call-start = ((), (), s32[]{:S(2)}) async-start(), calls=%async_computation.2 | async-start | bytes 16777216 | tf_op jit(solution)/shard_map/psum | solution.py:66
  504.5 1.6 copy-start.1
  504.5 2.2 copy-start.7
  665.8 4.9 copy-start.3
Sparse Core Ops, SparseCore 0:
  316.7 111.8 all-gather.1
  504.6 161.1 all-reduce.2
where the time goes:
time: 681 us; the launch traced here: 680 us
  local copies, waits for them, and re-layouts  318 us (47%)
  waiting for transfers between devices  260 us (38%)
  other arithmetic  44.2 us (6%)
  blocking collectives  26.6 us (4%)
  matrix products  16 us (2%)
  between operations  14.2 us (2%)
    gather x1, local copies, waits for them, and re-layouts, shards(): gathered = jnp.take(node_rows, neighbours.reshape(-1), axis=0, mode='clip')  208 us
    psum x1, waiting for transfers between devices, shards(): lax.psum((grad_self, grad_neighbour), ('feat', 'dom'))  157 us
    all_gather x1, waiting for transfers between devices, shards(): segment = lax.all_gather(layer_out, 'dom', axis=0, tiled=True)  103 us
    gather x1, local copies, waits for them, and re-layouts, shards(): fetched = jnp.take(segment, flat_rows.reshape(-1), axis=0, mode='clip')  33.7 us
    all_to_all x1, blocking collectives, shards(): arrived = lax.all_to_all(both, 'feat', 0, 0, tiled=True)  26.6 us
    convert_element_type x1, local copies, waits for them, and re-layouts, shards(): jnp.sum(gathered.reshape(targets_part, fanout_first, columns_here), axis=...  26.1 us
    reduce_sum x1, other arithmetic, shards(): jnp.sum(gathered.reshape(targets_part, fanout_first, columns_here), axis=...  25.2 us
    convert_element_type x1, local copies, waits for them, and re-layouts, shards(): jnp.sum(fetched.reshape(seed_rows, fanout_second, hidden_width), axis=1,...  21.4 us
  transfers between devices with their start and end apart: 2, of which 2 were waited for; matrix products, arithmetic and copies ran while one was open for 2% of the time, Pallas kernels for 0%

commit v1 on v0

--- a/solution.py
+++ b/solution.py
@@ -2,6 +2,12 @@
 import jax.numpy as jnp
 from jax import lax
 from jax.sharding import PartitionSpec as P
+
+
+def laid_out(tiles, dim):
+    dims = list(tiles.shape[1:])
+    dims[dim] *= tiles.shape[0]
+    return jnp.moveaxis(tiles, 0, dim).reshape(dims)
 
 
 def contract(left, right):
@@ -50,7 +56,19 @@
     layer_out = jnp.maximum(pre_first, 0.0).astype(jnp.bfloat16)
     seed_rows = cotangent.shape[0]
     fanout_second = offsets.shape[1]
-    segment = lax.all_gather(layer_out, "dom", axis=0, tiled=True)
+    devices = lax.axis_size("dom")
+    pairs = [(i, (i + 1) % devices) for i in range(devices)]
+    back = [(b, a) for a, b in pairs]
+    lower, upper = ([], [])
+    for lap in range(devices - 1):
+        if lap % 2 == 0:
+            lower.append(lax.ppermute(lower[-1] if lower else layer_out, "dom", pairs))
+        else:
+            upper.append(lax.ppermute(upper[-1] if upper else layer_out, "dom", back))
+    blocks = jnp.stack([*lower[::-1], layer_out, *upper])
+    shift = lax.axis_index("dom") - len(lower)
+    blocks = blocks[(jnp.arange(devices) - shift) % devices]
+    segment = laid_out(blocks, 0)
     flat_rows = owners.reshape(seed_rows, fanout_second) * share_rows + offsets
     fetched = jnp.take(segment, flat_rows.reshape(-1), axis=0, mode="clip")
     summed = jnp.sum(

time: 681 us -> 808 us (1.19)
  waiting for transfers between devices: 260 us -> 310 us
  local copies, waits for them, and re-layouts: 318 us -> 354 us
  starting transfers between devices: 0.26 us -> 36.2 us
    ppermute x0 -> x15, waiting for transfers between devices: none -> 150 us  [the longest x8 150 us: shards(): lower.append(lax.ppermute(lower[-1] if lower else layer_out, 'dom', pairs))]
    all_gather x1 -> x0, waiting for transfers between devices: 103 us -> none  [shards(): segment = lax.all_gather(layer_out, 'dom', axis=0, tiled=True)]
    ppermute x0 -> x15, starting transfers between devices: none -> 36.1 us  [the longest x7 34.9 us: shards(): upper.append(lax.ppermute(upper[-1] if upper else layer_out, 'dom', back))]
    unnamed x26 -> x69, local copies, waits for them, and re-layouts: 18.6 us -> 39.1 us
    gather x0 -> x1, local copies, waits for them, and re-layouts: none -> 13 us  [shards(): blocks = blocks[(jnp.arange(devices) - shift) % devices]]
  transfers between devices with their start and end apart: 2 -> 16, of which waited for: 2 -> 9; matrix products, arithmetic and copies ran while one was open for 2% -> 4% of each run, Pallas kernels for 0% -> 0%
where the time goes in v1:
time: 808 us; the launch traced here: 806 us
  local copies, waits for them, and re-layouts  354 us (44%)
  waiting for transfers between devices  310 us (38%)
  other arithmetic  45.6 us (6%)
  starting transfers between devices  36.2 us (4%)
  blocking collectives  26.3 us (3%)
  matrix products  19.2 us (2%)
  between operations  14.3 us (2%)
    gather x1, local copies, waits for them, and re-layouts, shards(): gathered = jnp.take(node_rows, neighbours.reshape(-1), axis=0, mode='clip')  209 us
    psum x1, waiting for transfers between devices, shards(): lax.psum((grad_self, grad_neighbour), ('feat', 'dom'))  160 us
    ppermute x8, waiting for transfers between devices, shards(): lower.append(lax.ppermute(lower[-1] if lower else layer_out, 'dom', pairs))  150 us
    unnamed x69, local copies, waits for them, and re-layouts  39.1 us
    ppermute x7, starting transfers between devices, shards(): upper.append(lax.ppermute(upper[-1] if upper else layer_out, 'dom', back))  34.9 us
    gather x1, local copies, waits for them, and re-layouts, shards(): fetched = jnp.take(segment, flat_rows.reshape(-1), axis=0, mode='clip')  33.8 us
    all_to_all x1, blocking collectives, shards(): arrived = lax.all_to_all(both, 'feat', 0, 0, tiled=True)  26.3 us
    convert_element_type x1, local copies, waits for them, and re-layouts, shards(): jnp.sum(gathered.reshape(targets_part, fanout_first, columns_here), axis=...  26.1 us
  transfers between devices with their start and end apart: 16, of which 9 were waited for; matrix products, arithmetic and copies ran while one was open for 4% of the time, Pallas kernels for 0%

profile of v1, /device:TPU:1, one launch (start us, length us, event | category | flops | bytes accessed | tf_op | source)
XLA Modules:
  0.0 805.8 jit_solution(9287065512135525611)
XLA Ops:
  7.2 6.0 copy.26
  13.2 2.9 copy.28
  16.1 3.2 reshape.99
  19.4 1.3 slice.10
  20.7 208.5 %gather_fusion = bf16[61440,96]{1,0:T(8,128)(2,1)} fusion(bf16[16384,96]{1,0:T(8,128)(2,1)} %bitcast.60, s32[61440]{0:T(1024)S(1)} %broadcast_clamp_fusion), kind=kCustom, calls=%fused_computation | custom fusion | bytes 23838720 | tf_op jit(solution)/shard_map/jit(_take)/gather | solution.py:37
  229.2 26.1 %reshape.95 = f32[4096,15,96]{2,1,0:T(8,128)} reshape(bf16[61440,96]{1,0:T(8,128)(2,1)} %gather_fusion) | data formatting | bytes 35389440 | tf_op jit(solution)/shard_map/convert_element_type | solution.py:39
  255.3 25.2 %reduce_sum.18 = f32[4096,96]{1,0:T(8,128)} reduce(f32[4096,15,96]{2,1,0:T(8,128)} %reshape.95, f32[]{:T(128)} %constant.12.clone.1), dimensions={1}, to_apply=%region_0.1 | reduce | flops 5505024 | bytes 25165828 | tf_op jit(solution)/shard_map/reduce_sum | solution.py:39
  280.4 2.8 copy.29
  283.2 1.5 multiply_convert_fusion.1
  285.1 1.1 copy.31
  286.2 1.2 copy.30
  287.4 1.5 pad_maximum_fusion
  288.9 26.3 %all_to_all.5 = bf16[8,512,2,96]{1,3,2,0:T(8,128)(2,1)S(1)} all-to-all(bf16[8,512,2,96]{1,3,2,0:T(8,128)(2,1)S(1)} %pad_maximum_fusion), channel_id=1, replica_groups=mesh['feat'=8,'dom'=16] {'feat'}, dimensions={0} | all-to-all | bytes 3145728 | tf_op jit(solution)/shard_map/all_to_all | solution.py:46
  315.3 3.7 fusion.4
  318.9 1.3 collective-permute-start
  320.2 27.2 %collective-permute-done = bf16[512,1024]{1,0:T(8,128)(2,1)S(1)} collective-permute-done((bf16[512,1024]{1,0:T(8,128)(2,1)S(1)}, bf16[512,1024]{1,0:T(8,128)(2,1)S(1)}, u32[]{:S(2)}, u32[]{:S(2)}) %collective-permute-start) | collective-permute-done | bytes 1048608 | tf_op jit(solution)/shard_map/ppermute | solution.py:65
  347.5 4.8 collective-permute-start.8
  352.2 21.6 %collective-permute-done.1 = bf16[512,1024]{1,0:T(8,128)(2,1)S(1)} collective-permute-done((bf16[512,1024]{1,0:T(8,128)(2,1)S(1)}, bf16[512,1024]{1,0:T(8,128)(2,1)S(1)}, u32[]{:S(2)}, u32[]{:S(2)}) %collective-permute-start.1) | collective-permute-done | bytes 1048608 | tf_op jit(solution)/shard_map/ppermute | solution.py:65
  373.9 4.8 collective-permute-start.9
  378.7 20.7 %collective-permute-done.2 = bf16[512,1024]{1,0:T(8,128)(2,1)S(1)} collective-permute-done((bf16[512,1024]{1,0:T(8,128)(2,1)S(1)}, bf16[512,1024]{1,0:T(8,128)(2,1)S(1)}, u32[]{:S(2)}, u32[]{:S(2)}) %collective-permute-start.2) | collective-permute-done | bytes 1048608 | tf_op jit(solution)/shard_map/ppermute | solution.py:65
  399.5 5.0 collective-permute-start.10
  404.5 19.7 %collective-permute-done.3 = bf16[512,1024]{1,0:T(8,128)(2,1)S(1)} collective-permute-done((bf16[512,1024]{1,0:T(8,128)(2,1)S(1)}, bf16[512,1024]{1,0:T(8,128)(2,1)S(1)}, u32[]{:S(2)}, u32[]{:S(2)}) %collective-permute-start.3) | collective-permute-done | bytes 1048608 | tf_op jit(solution)/shard_map/ppermute | solution.py:65
  424.2 4.8 collective-permute-start.11
  429.0 19.0 %collective-permute-done.4 = bf16[512,1024]{1,0:T(8,128)(2,1)S(1)} collective-permute-done((bf16[512,1024]{1,0:T(8,128)(2,1)S(1)}, bf16[512,1024]{1,0:T(8,128)(2,1)S(1)}, u32[]{:S(2)}, u32[]{:S(2)}) %collective-permute-start.4) | collective-permute-done | bytes 1048608 | tf_op jit(solution)/shard_map/ppermute | solution.py:65
  449.1 4.8 collective-permute-start.12
  453.8 17.2 %collective-permute-done.5 = bf16[512,1024]{1,0:T(8,128)(2,1)S(1)} collective-permute-done((bf16[512,1024]{1,0:T(8,128)(2,1)S(1)}, bf16[512,1024]{1,0:T(8,128)(2,1)S(1)}, u32[]{:S(2)}, u32[]{:S(2)}) %collective-permute-start.5) | collective-permute-done | bytes 1048608 | tf_op jit(solution)/shard_map/ppermute | solution.py:65
  471.0 5.6 collective-permute-start.13
  476.6 16.6 %collective-permute-done.6 = bf16[512,1024]{1,0:T(8,128)(2,1)} collective-permute-done((bf16[512,1024]{1,0:T(8,128)(2,1)S(1)}, bf16[512,1024]{1,0:T(8,128)(2,1)}, u32[]{:S(2)}, u32[]{:S(2)}) %collective-permute-start.6) | collective-permute-done | bytes 1048608 | tf_op jit(solution)/shard_map/ppermute | solution.py:65
  494.4 1.7 add.36
  496.1 1.1 reshape.115
  497.3 4.7 fusion.15
  502.0 5.1 collective-permute-start.14
  507.1 7.8 collective-permute-done.7
  514.9 2.3 bitcast_dynamic-update-slice_fusion.15
  517.2 2.4 bitcast_dynamic-update-slice_fusion.14
  524.8 1.1 bitcast_dynamic-update-slice_fusion.8
  531.3 2.3 bitcast_dynamic-update-slice_fusion.2
  533.6 2.3 bitcast_dynamic-update-slice_fusion.1
  537.0 13.0 %gather_fusion.1 = bf16[16,512,1024]{2,1,0:T(8,128)(2,1)} fusion(bf16[16,512,1024]{2,1,0:T(8,128)(2,1)} %bitcast_dynamic-update-slice_fusion, s32[1024]{0:T(1024)S(1)} %pad_clamp_fusion), kind=kCustom, calls=%fused_computation.1 | custom fusion | bytes 33554496 | tf_op jit(solution)/shard_map/gather | solution.py:70
  550.0 33.8 %gather_fusion.2 = bf16[5120,1024]{1,0:T(8,128)(2,1)} fusion(bf16[8192,1024]{1,0:T(8,128)(2,1)} %bitcast.61, s32[5120]{0:T(1024)S(1)} %broadcast_clamp_fusion.1), kind=kCustom, calls=%fused_computation.2 | custom fusion | bytes 20992000 | tf_op jit(solution)/shard_map/jit(_take)/gather | solution.py:73
  583.8 21.5 %reshape.96 = f32[512,10,1024]{2,1,0:T(8,128)} reshape(bf16[5120,1024]{1,0:T(8,128)(2,1)} %gather_fusion.2) | data formatting | bytes 31457280 | tf_op jit(solution)/shard_map/convert_element_type | solution.py:74
  605.3 15.6 %reduce_sum.19 = f32[512,1024]{1,0:T(8,128)} reduce(f32[512,10,1024]{2,1,0:T(8,128)} %reshape.96, f32[]{:T(128)} %constant.12.clone.1), dimensions={1}, to_apply=%region_1.2 | reduce | flops 4718592 | bytes 23068676 | tf_op jit(solution)/shard_map/reduce_sum | solution.py:74
  620.8 5.2 fusion.8
  626.0 1.3 fusion.14
  627.3 4.5 add_convert_fusion
  631.7 160.2 %all-reduce.3.cloned.1.call-done = (f32[1024,1024]{1,0:T(8,128)}, f32[1024,1024]{1,0:T(8,128)}) async-done(((f32[1024,1024]{1,0:T(8,128)}, f32[1024,1024]{1,0:T(8,128)}), (f32[1024,1024]{1,0:T(8,128)}, f32[1024,1024]{1,0:T(8,128)})) %all-reduce.3.cloned.1.call-update) | async-done | bytes 8388624 | tf_op jit(solution)/shard_map/psum | solution.py:84
  792.0 4.9 copy.54
  796.9 2.0 copy.55
  (83 shorter events, 14.4 us)
Async XLA Ops:
  7.2 618.9 %copy-start = (bf16[1024,1024]{1,0:T(8,128)(2,1)S(1)}, bf16[1024,1024]{1,0:T(8,128)(2,1)}, u32[]{:S(2)}) copy-start(bf16[1024,1024]{1,0:T(8,128)(2,1)} %param.15) | copy-start | bytes 6291460
  7.2 784.8 %all-reduce.3.cloned.1.call-start = ((), (), s32[]{:S(2)}) async-start(), calls=%async_computation.1 | async-start | bytes 16777216 | tf_op jit(solution)/shard_map/psum | solution.py:84
  283.2 210.1 %copy-start.23 = (s32[5120,1]{0,1:T(1,128)S(1)}, s32[5120,1]{0,1:T(1,128)}, u32[]{:S(2)}) copy-start(s32[5120,1]{0,1:T(1,128)} %param.13) | copy-start | bytes 61444
  284.8 208.8 %copy-start.22 = (s32[512,10]{0,1:T(8,128)S(1)}, s32[512,10]{0,1:T(8,128)}, u32[]{:S(2)}) copy-start(s32[512,10]{0,1:T(8,128)} %param.14) | copy-start | bytes 61444
  318.9 28.5 %collective-permute-start = (bf16[512,1024]{1,0:T(8,128)(2,1)S(1)}, bf16[512,1024]{1,0:T(8,128)(2,1)S(1)}, u32[]{:S(2)}, u32[]{:S(2)}) collective-permute-start(bf16[512,1024]{1,0:T(8,128)(2,1)S(1)} %fusion.4), channel_id=1, source_target_pairs={{0,1},{1,2},{2,3},{3,4},{4,5},{5,6},{6,7},{7,8},{8,9},{9,10},{10,1... | collective-permute-start | bytes 3145736 | tf_op jit(solution)/shard_map/ppermute | solution.py:65
  347.5 26.4 %copy-start.2 = (bf16[512,1024]{1,0:T(8,128)(2,1)}, bf16[512,1024]{1,0:T(8,128)(2,1)S(1)}, u32[]{:S(2)}) copy-start(bf16[512,1024]{1,0:T(8,128)(2,1)S(1)} %collective-permute-done) | copy-start | bytes 3145732
  347.5 26.4 %collective-permute-start.1 = (bf16[512,1024]{1,0:T(8,128)(2,1)S(1)}, bf16[512,1024]{1,0:T(8,128)(2,1)S(1)}, u32[]{:S(2)}, u32[]{:S(2)}) collective-permute-start(bf16[512,1024]{1,0:T(8,128)(2,1)S(1)} %collective-permute-done), channel_id=1, source_target_pairs={{0,1},{1,2},{2,3},{3,4},{4,5},{5,6},{6,7},{7,8},{8,9},{9,10},{10,1... | collective-permute-start | bytes 3145736 | tf_op jit(solution)/shard_map/ppermute | solution.py:65
  347.5 26.4 %collective-permute-start.8 = (bf16[512,1024]{1,0:T(8,128)(2,1)S(1)}, bf16[512,1024]{1,0:T(8,128)(2,1)S(1)}, u32[]{:S(2)}, u32[]{:S(2)}) collective-permute-start(bf16[512,1024]{1,0:T(8,128)(2,1)S(1)} %fusion.4), channel_id=1, source_target_pairs={{1,0},{2,1},{3,2},{4,3},{5,4},{6,5},{7,6},{8,7},{9,8},{10,9},{11,1... | collective-permute-start | bytes 3145736 | tf_op jit(solution)/shard_map/ppermute | solution.py:67
  373.9 25.6 %copy-start.6 = (bf16[512,1024]{1,0:T(8,128)(2,1)}, bf16[512,1024]{1,0:T(8,128)(2,1)S(1)}, u32[]{:S(2)}) copy-start(bf16[512,1024]{1,0:T(8,128)(2,1)S(1)} %collective-permute-done.1) | copy-start | bytes 3145732
  373.9 25.6 %collective-permute-start.2 = (bf16[512,1024]{1,0:T(8,128)(2,1)S(1)}, bf16[512,1024]{1,0:T(8,128)(2,1)S(1)}, u32[]{:S(2)}, u32[]{:S(2)}) collective-permute-start(bf16[512,1024]{1,0:T(8,128)(2,1)S(1)} %collective-permute-done.1), channel_id=1, source_target_pairs={{0,1},{1,2},{2,3},{3,4},{4,5},{5,6},{6,7},{7,8},{8,9},{9,10},{10,1... | collective-permute-start | bytes 3145736 | tf_op jit(solution)/shard_map/ppermute | solution.py:65
  373.9 4.8 copy-start.4
  373.9 25.5 %collective-permute-start.9 = (bf16[512,1024]{1,0:T(8,128)(2,1)S(1)}, bf16[512,1024]{1,0:T(8,128)(2,1)S(1)}, u32[]{:S(2)}, u32[]{:S(2)}) collective-permute-start(bf16[512,1024]{1,0:T(8,128)(2,1)S(1)} %collective-permute-done.8), channel_id=1, source_target_pairs={{1,0},{2,1},{3,2},{4,3},{5,4},{6,5},{7,6},{8,7},{9,8},{10,9},{11,1... | collective-permute-start | bytes 3145736 | tf_op jit(solution)/shard_map/ppermute | solution.py:67
  399.4 24.7 %copy-start.10 = (bf16[512,1024]{1,0:T(8,128)(2,1)}, bf16[512,1024]{1,0:T(8,128)(2,1)S(1)}, u32[]{:S(2)}) copy-start(bf16[512,1024]{1,0:T(8,128)(2,1)S(1)} %collective-permute-done.2) | copy-start | bytes 3145732
  399.4 24.7 %collective-permute-start.3 = (bf16[512,1024]{1,0:T(8,128)(2,1)S(1)}, bf16[512,1024]{1,0:T(8,128)(2,1)S(1)}, u32[]{:S(2)}, u32[]{:S(2)}) collective-permute-start(bf16[512,1024]{1,0:T(8,128)(2,1)S(1)} %collective-permute-done.2), channel_id=1, source_target_pairs={{0,1},{1,2},{2,3},{3,4},{4,5},{5,6},{6,7},{7,8},{8,9},{9,10},{10,1... | collective-permute-start | bytes 3145736 | tf_op jit(solution)/shard_map/ppermute | solution.py:65
  399.5 5.0 copy-start.8
  399.5 24.7 %collective-permute-start.10 = (bf16[512,1024]{1,0:T(8,128)(2,1)S(1)}, bf16[512,1024]{1,0:T(8,128)(2,1)S(1)}, u32[]{:S(2)}, u32[]{:S(2)}) collective-permute-start(bf16[512,1024]{1,0:T(8,128)(2,1)S(1)} %collective-permute-done.9), channel_id=1, source_target_pairs={{1,0},{2,1},{3,2},{4,3},{5,4},{6,5},{7,6},{8,7},{9,8},{10,9},{11,1... | collective-permute-start | bytes 3145736 | tf_op jit(solution)/shard_map/ppermute | solution.py:67
  424.2 46.9 %copy-start.16 = (bf16[512,1024]{1,0:T(8,128)(2,1)}, bf16[512,1024]{1,0:T(8,128)(2,1)S(1)}, u32[]{:S(2)}) copy-start(bf16[512,1024]{1,0:T(8,128)(2,1)S(1)} %collective-permute-done.3) | copy-start | bytes 3145732
  424.2 23.9 %collective-permute-start.4 = (bf16[512,1024]{1,0:T(8,128)(2,1)S(1)}, bf16[512,1024]{1,0:T(8,128)(2,1)S(1)}, u32[]{:S(2)}, u32[]{:S(2)}) collective-permute-start(bf16[512,1024]{1,0:T(8,128)(2,1)S(1)} %collective-permute-done.3), channel_id=1, source_target_pairs={{0,1},{1,2},{2,3},{3,4},{4,5},{5,6},{6,7},{7,8},{8,9},{9,10},{10,1... | collective-permute-start | bytes 3145736 | tf_op jit(solution)/shard_map/ppermute | solution.py:65
  424.2 4.8 copy-start.12
  424.2 23.8 %collective-permute-start.11 = (bf16[512,1024]{1,0:T(8,128)(2,1)S(1)}, bf16[512,1024]{1,0:T(8,128)(2,1)S(1)}, u32[]{:S(2)}, u32[]{:S(2)}) collective-permute-start(bf16[512,1024]{1,0:T(8,128)(2,1)S(1)} %collective-permute-done.10), channel_id=1, source_target_pairs={{1,0},{2,1},{3,2},{4,3},{5,4},{6,5},{7,6},{8,7},{9,8},{10,9},{11,1... | collective-permute-start | bytes 3145736 | tf_op jit(solution)/shard_map/ppermute | solution.py:67
  448.0 28.6 %copy-start.18 = (bf16[512,1024]{1,0:T(8,128)(2,1)}, bf16[512,1024]{1,0:T(8,128)(2,1)S(1)}, u32[]{:S(2)}) copy-start(bf16[512,1024]{1,0:T(8,128)(2,1)S(1)} %collective-permute-done.4) | copy-start | bytes 3145732
  448.0 23.0 %collective-permute-start.5 = (bf16[512,1024]{1,0:T(8,128)(2,1)S(1)}, bf16[512,1024]{1,0:T(8,128)(2,1)S(1)}, u32[]{:S(2)}, u32[]{:S(2)}) collective-permute-start(bf16[512,1024]{1,0:T(8,128)(2,1)S(1)} %collective-permute-done.4), channel_id=1, source_target_pairs={{0,1},{1,2},{2,3},{3,4},{4,5},{5,6},{6,7},{7,8},{8,9},{9,10},{10,1... | collective-permute-start | bytes 3145736 | tf_op jit(solution)/shard_map/ppermute | solution.py:65
  448.0 1.0 copy-start.14
  449.1 22.0 %collective-permute-start.12 = (bf16[512,1024]{1,0:T(8,128)(2,1)S(1)}, bf16[512,1024]{1,0:T(8,128)(2,1)}, u32[]{:S(2)}, u32[]{:S(2)}) collective-permute-start(bf16[512,1024]{1,0:T(8,128)(2,1)S(1)} %collective-permute-done.11), channel_id=1, source_target_pairs={{1,0},{2,1},{3,2},{4,3},{5,4},{6,5},{7,6},{8,7},{9,8},{10,9},{11,1... | collective-permute-start | bytes 3145736 | tf_op jit(solution)/shard_map/ppermute | solution.py:67
  471.0 22.3 %copy-start.20 = (bf16[512,1024]{1,0:T(8,128)(2,1)}, bf16[512,1024]{1,0:T(8,128)(2,1)S(1)}, u32[]{:S(2)}) copy-start(bf16[512,1024]{1,0:T(8,128)(2,1)S(1)} %collective-permute-done.5) | copy-start | bytes 3145732
  471.0 22.2 %collective-permute-start.6 = (bf16[512,1024]{1,0:T(8,128)(2,1)S(1)}, bf16[512,1024]{1,0:T(8,128)(2,1)}, u32[]{:S(2)}, u32[]{:S(2)}) collective-permute-start(bf16[512,1024]{1,0:T(8,128)(2,1)S(1)} %collective-permute-done.5), channel_id=1, source_target_pairs={{0,1},{1,2},{2,3},{3,4},{4,5},{5,6},{6,7},{7,8},{8,9},{9,10},{10,1... | collective-permute-start | bytes 3145736 | tf_op jit(solution)/shard_map/ppermute | solution.py:65
  471.0 31.0 %collective-permute-start.13 = (bf16[512,1024]{1,0:T(8,128)(2,1)}, bf16[512,1024]{1,0:T(8,128)(2,1)}, u32[]{:S(2)}, u32[]{:S(2)}) collective-permute-start(bf16[512,1024]{1,0:T(8,128)(2,1)} %collective-permute-done.12), channel_id=1, source_target_pairs={{1,0},{2,1},{3,2},{4,3},{5,4},{6,5},{7,6},{8,7},{9,8},{10,9},{11,1... | collective-permute-start | bytes 3145736 | tf_op jit(solution)/shard_map/ppermute | solution.py:67
  493.3 21.6 %collective-permute-start.7 = (bf16[512,1024]{1,0:T(8,128)(2,1)}, bf16[512,1024]{1,0:T(8,128)(2,1)}, u32[]{:S(2)}, u32[]{:S(2)}) collective-permute-start(bf16[512,1024]{1,0:T(8,128)(2,1)} %collective-permute-done.6), channel_id=1, source_target_pairs={{0,1},{1,2},{2,3},{3,4},{4,5},{5,6},{6,7},{7,8},{8,9},{9,10},{10,1... | collective-permute-start | bytes 3145736 | tf_op jit(solution)/shard_map/ppermute | solution.py:65
  497.2 22.3 %copy-start.21 = (bf16[512,1024]{1,0:T(8,128)(2,1)S(1)}, bf16[512,1024]{1,0:T(8,128)(2,1)}, u32[]{:S(2)}) copy-start(bf16[512,1024]{1,0:T(8,128)(2,1)} %copy-done.20) | copy-start | bytes 3145732
  497.2 23.3 %copy-start.19 = (bf16[512,1024]{1,0:T(8,128)(2,1)S(1)}, bf16[512,1024]{1,0:T(8,128)(2,1)}, u32[]{:S(2)}) copy-start(bf16[512,1024]{1,0:T(8,128)(2,1)} %copy-done.18) | copy-start | bytes 3145732
  497.2 24.4 %copy-start.17 = (bf16[512,1024]{1,0:T(8,128)(2,1)S(1)}, bf16[512,1024]{1,0:T(8,128)(2,1)}, u32[]{:S(2)}) copy-start(bf16[512,1024]{1,0:T(8,128)(2,1)} %copy-done.16) | copy-start | bytes 3145732
  497.3 25.5 %copy-start.11 = (bf16[512,1024]{1,0:T(8,128)(2,1)S(1)}, bf16[512,1024]{1,0:T(8,128)(2,1)}, u32[]{:S(2)}) copy-start(bf16[512,1024]{1,0:T(8,128)(2,1)} %copy-done.10) | copy-start | bytes 3145732
  497.3 26.5 %copy-start.7 = (bf16[512,1024]{1,0:T(8,128)(2,1)S(1)}, bf16[512,1024]{1,0:T(8,128)(2,1)}, u32[]{:S(2)}) copy-start(bf16[512,1024]{1,0:T(8,128)(2,1)} %copy-done.6) | copy-start | bytes 3145732
  497.3 27.5 %copy-start.3 = (bf16[512,1024]{1,0:T(8,128)(2,1)S(1)}, bf16[512,1024]{1,0:T(8,128)(2,1)}, u32[]{:S(2)}) copy-start(bf16[512,1024]{1,0:T(8,128)(2,1)} %copy-done.2) | copy-start | bytes 3145732
  502.0 25.0 %copy-start.5 = (bf16[512,1024]{1,0:T(8,128)(2,1)S(1)}, bf16[512,1024]{1,0:T(8,128)(2,1)}, u32[]{:S(2)}) copy-start(bf16[512,1024]{1,0:T(8,128)(2,1)} %copy-done.4) | copy-start | bytes 3145732
  502.0 26.1 %copy-start.9 = (bf16[512,1024]{1,0:T(8,128)(2,1)S(1)}, bf16[512,1024]{1,0:T(8,128)(2,1)}, u32[]{:S(2)}) copy-start(bf16[512,1024]{1,0:T(8,128)(2,1)} %copy-done.8) | copy-start | bytes 3145732
  502.0 33.9 %collective-permute-start.14 = (bf16[512,1024]{1,0:T(8,128)(2,1)}, bf16[512,1024]{1,0:T(8,128)(2,1)S(1)}, u32[]{:S(2)}, u32[]{:S(2)}) collective-permute-start(bf16[512,1024]{1,0:T(8,128)(2,1)} %collective-permute-done.13), channel_id=1, source_target_pairs={{1,0},{2,1},{3,2},{4,3},{5,4},{6,5},{7,6},{8,7},{9,8},{10,9},{11,1... | collective-permute-start | bytes 3145736 | tf_op jit(solution)/shard_map/ppermute | solution.py:67
  517.2 12.0 %copy-start.13 = (bf16[512,1024]{1,0:T(8,128)(2,1)S(1)}, bf16[512,1024]{1,0:T(8,128)(2,1)}, u32[]{:S(2)}) copy-start(bf16[512,1024]{1,0:T(8,128)(2,1)} %copy-done.12) | copy-start | bytes 3145732
  519.5 10.7 %copy-start.15 = (bf16[512,1024]{1,0:T(8,128)(2,1)S(1)}, bf16[512,1024]{1,0:T(8,128)(2,1)}, u32[]{:S(2)}) copy-start(bf16[512,1024]{1,0:T(8,128)(2,1)} %copy-done.14) | copy-start | bytes 3145732
  792.0 4.9 copy-start.1
Sparse Core Ops, SparseCore 0:
  626.1 165.7 all-reduce.2
